TPU v7x, 256 devices: a whole 4x4x8 slice. The times are simulated.
256 devices in a mesh: seq: 64 (over x, z, core), head: 4 (over y).
Axes of the slice: x: 4, y: 4, z: 8, core: 2. Of those that a mesh axis runs over, the one named last changes fastest.
Arguments:
- queries: bfloat16 [16384, 2048], P('seq', 'head'), may hold values from -30 to 30, as said below
- keys: bfloat16 [16384, 2048], P('seq', 'head'), may hold values from -30 to 30, as said below
- values: bfloat16 [16384, 2048], P('seq', 'head'), may hold values from -6 to 6
- out_grad: bfloat16 [16384, 2048], P('seq', 'head'), may hold values from -6 to 6
- rand_blocks: int32 [16, 128, 3], P('head', 'seq'), may hold values from 0 to 127, as said below
Outputs:
- attn_out: bfloat16 [16384, 2048], P('seq', 'head')
- grad_queries: bfloat16 [16384, 2048], P('seq', 'head')
- grad_keys: bfloat16 [16384, 2048], P('seq', 'head')
- grad_values: bfloat16 [16384, 2048], P('seq', 'head')
Inputs may be any that keep to these rules, and one draw needn't show every extreme that they name: queries are of order one; in some draws a few rows reach larger scales. keys are of order one; in some draws a few rows reach larger scales. `rand_blocks`: for each aligned group of 4 heads and each aligned run of 2 query blocks, at most 2 of the group's entries name blocks of one aligned run of 2 key blocks, and in every group some run is named exactly 2 times.
All inputs are finite; a program needn't handle non-finite values.
Results may differ from a plain program's by a relative error of at most 0.015.
The roundings to bfloat16 on the way count: a program that leaves them out, or rounds other values in their place, can miss the bound.
Values may be sent and summed in bfloat16 or wider, within the bound.
No kernel may reach another device: no remote copies, remote signals or barrier semaphores. Data moves between devices by JAX's collectives and lax.ppermute only.
A program may use at most 192 MiB of HBM per device.

v0:
```python
import math

import jax
import jax.numpy as jnp
from jax import lax
from jax.experimental.layout import Layout, with_layout_constraint
from jax.sharding import PartitionSpec as P


def swapped(value, axis, distance):
    mask = 2**distance
    pairs = [(source, source ^ mask) for source in range(lax.axis_size(axis))]
    return lax.ppermute(value, axis, pairs)


def low(value_arr):
    return value_arr.astype(jnp.bfloat16).astype(jnp.float32)


def body(queries, keys, values, out_grad, rand_blocks):
    tok_rows = queries.shape[0]
    heads_here, blk_count, rand_count = rand_blocks.shape
    head_size = queries.shape[1] // heads_here
    blk_size = tok_rows // blk_count
    score_scale = 1.0 / math.sqrt(head_size)
    seq_devices = lax.axis_size("seq")
    far_count = seq_devices.bit_length() - 1
    f32 = jnp.float32

    def heads_first(arr):
        return arr.reshape(blk_count, blk_size, heads_here, head_size).transpose(2, 0, 1, 3)

    def rows_back(arr):
        return arr.transpose(1, 2, 0, 3).reshape(tok_rows, heads_here * head_size)

    total_req = heads_here * blk_count * rand_count
    slot_cap = max(2, -(-total_req // seq_devices))
    slot_count = seq_devices * slot_cap
    flat_req = rand_blocks.reshape(-1)
    owner_dev = flat_req // blk_count
    req_index = jnp.arange(total_req, dtype=jnp.int32)
    req_head = req_index // (blk_count * rand_count)
    payload = req_head * blk_count + flat_req % blk_count
    earlier_same = (owner_dev[:, None] == owner_dev[None, :]) & (
        req_index[:, None] > req_index[None, :]
    )
    slot_rank = jnp.sum(earlier_same.astype(jnp.int32), axis=1)
    slot_of_req = owner_dev * slot_cap + slot_rank
    slot_match = slot_of_req[None, :] == jnp.arange(slot_count, dtype=jnp.int32)[:, None]
    filled = jnp.any(slot_match, axis=1)
    send_ids = jnp.where(filled, jnp.sum(jnp.where(slot_match, payload[None, :], 0), axis=1), -1)
    asked_ids = lax.all_to_all(
        send_ids.reshape(seq_devices, slot_cap), "seq", split_axis=0, concat_axis=0, tiled=True
    )
    asked_flat = asked_ids.reshape(-1)

    kv_rows = jnp.stack([keys, values])
    far_kv = [swapped(kv_rows, "seq", far_level) for far_level in range(far_count)]

    kv_four = kv_rows.reshape(2, blk_count, blk_size, heads_here, head_size)
    safe_ids = jnp.maximum(asked_flat, 0)
    pick_head = safe_ids // blk_count
    pick_blk = safe_ids % blk_count
    kv_pick = kv_four[:, pick_blk, :, pick_head, :]
    kv_back = lax.all_to_all(
        kv_pick.reshape(seq_devices, slot_cap, 2, blk_size, head_size),
        "seq",
        split_axis=0,
        concat_axis=0,
        tiled=True,
    ).reshape(slot_count, 2, blk_size, head_size)
    rand_kv = kv_back[slot_of_req].reshape(
        heads_here, blk_count, rand_count, 2, blk_size, head_size
    )

    def fixed_list(which):
        own = heads_first(kv_rows[which])
        parts = [own[:, :, None], own[:, ::-1, None]]
        parts += [heads_first(far_arr[which])[:, :, None] for far_arr in far_kv]
        return jnp.concatenate(parts, axis=2)

    key_fix = fixed_list(0)
    value_fix = fixed_list(1)
    key_rnd = rand_kv[:, :, :, 0]
    value_rnd = rand_kv[:, :, :, 1]
    query_h = heads_first(queries)
    grad_h = heads_first(out_grad)

    def mm_scores(rows, key_part):
        return jnp.einsum("hbtd,hbksd->hbtks", rows, key_part, preferred_element_type=f32)

    def mm_out(weight_part, key_part):
        return jnp.einsum("hbtks,hbksd->hbtd", weight_part, key_part, preferred_element_type=f32)

    def mm_terms(weight_part, rows):
        return jnp.einsum("hbtks,hbtd->hbksd", weight_part, rows, preferred_element_type=f32)

    scores_fix = mm_scores(query_h, key_fix) * score_scale
    scores_rnd = mm_scores(query_h, key_rnd) * score_scale
    grad_weights_fix = mm_scores(grad_h, value_fix)
    grad_weights_rnd = mm_scores(grad_h, value_rnd)
    row_max = jnp.maximum(jnp.max(scores_fix, axis=(3, 4)), jnp.max(scores_rnd, axis=(3, 4)))
    exp_sum = jnp.sum(jnp.exp(scores_fix - row_max[..., None, None]), axis=(3, 4)) + jnp.sum(
        jnp.exp(scores_rnd - row_max[..., None, None]), axis=(3, 4)
    )
    log_total = row_max + jnp.log(exp_sum)
    weights_fix = jnp.exp(scores_fix - log_total[..., None, None])
    weights_rnd = jnp.exp(scores_rnd - log_total[..., None, None])
    low_fix = weights_fix.astype(jnp.bfloat16)
    low_rnd = weights_rnd.astype(jnp.bfloat16)
    attn_h = (mm_out(low_fix, value_fix) + mm_out(low_rnd, value_rnd)).astype(jnp.bfloat16)
    row_delta = jnp.sum(grad_h.astype(f32) * attn_h.astype(f32), axis=3)
    grad_scores_fix = (weights_fix * (grad_weights_fix - row_delta[..., None, None])).astype(
        jnp.bfloat16
    )
    grad_scores_rnd = (weights_rnd * (grad_weights_rnd - row_delta[..., None, None])).astype(
        jnp.bfloat16
    )

    rand_low = jnp.stack(
        [score_scale * mm_terms(grad_scores_rnd, query_h), mm_terms(low_rnd, grad_h)]
    ).astype(jnp.bfloat16)
    rand_req = rand_low.transpose(1, 2, 3, 0, 4, 5).reshape(total_req, 2, blk_size, head_size)
    rand_req = jnp.concatenate([rand_req, jnp.zeros_like(rand_req[:1])], axis=0)
    req_of_slot = jnp.where(
        jnp.any(slot_match, axis=1),
        jnp.sum(jnp.where(slot_match, req_index[None, :], 0), axis=1),
        total_req,
    )
    send_terms = rand_req[req_of_slot]
    row_major = Layout(major_to_minor=(0, 1, 2, 3, 4))
    slot_terms = lax.all_to_all(
        with_layout_constraint(
            send_terms.reshape(seq_devices, slot_cap, 2, blk_size, head_size), row_major
        ),
        "seq",
        split_axis=0,
        concat_axis=0,
        tiled=True,
    )
    slot_terms = with_layout_constraint(slot_terms, row_major).reshape(
        slot_count, 2, blk_size, head_size
    )

    grad_query_h = (
        score_scale * (mm_out(grad_scores_fix, key_fix) + mm_out(grad_scores_rnd, key_rnd))
    ).astype(jnp.bfloat16)
    terms = jnp.stack(
        [score_scale * mm_terms(grad_scores_fix, query_h), mm_terms(low_fix, grad_h)]
    )

    grad_kv = terms[:, :, :, 0] + low(terms[:, :, :, 1])[:, :, ::-1]
    far_low = terms[:, :, :, 2:].astype(jnp.bfloat16)
    for far_level in range(far_count):
        back = swapped(far_low[:, :, :, far_level], "seq", far_level)
        grad_kv = grad_kv + back.astype(f32)
    grad_rows = grad_kv.transpose(0, 2, 3, 1, 4)

    target_rows = jnp.arange(heads_here * blk_count, dtype=jnp.int32)
    onehot = (asked_flat[None, :] == target_rows[:, None]).astype(jnp.bfloat16)
    extra = jnp.einsum("tp,pksd->tksd", onehot, slot_terms, preferred_element_type=f32)
    extra = extra.reshape(heads_here, blk_count, 2, blk_size, head_size).transpose(2, 1, 3, 0, 4)
    grad_kv = (grad_rows + extra).astype(jnp.bfloat16).reshape(2, tok_rows, heads_here * head_size)

    attn_out = rows_back(attn_h)
    grad_queries = rows_back(grad_query_h)
    grad_keys = grad_kv[0]
    grad_values = grad_kv[1]
    return (attn_out, grad_queries, grad_keys, grad_values)


def solution(mesh):
    return jax.shard_map(
        body,
        mesh=mesh,
        in_specs=(
            P("seq", "head"),
            P("seq", "head"),
            P("seq", "head"),
            P("seq", "head"),
            P("head", "seq", None),
        ),
        out_specs=(P("seq", "head"), P("seq", "head"), P("seq", "head"), P("seq", "head")),
        check_vma=False,
    )
```

profile of v0, /device:TPU:152, one launch (start us, length us, event | category | flops | bytes accessed | tf_op | source)
XLA Modules:
  0.0 566.4 jit_solution(14812417555420278301)
XLA Ops:
  2.7 10.2 %all-to-all-start = ((s32[64,1,2]{2,1,0:T(1,128)}), s32[64,1,2]{2,1,0:T(1,128)S(1)}, u32[]{:S(2)}, u32[]{:S(2)}) async-start(s32[64,1,2]{2,1,0:T(1,128)} %bitcast.22), calls=%async_computation | async-start | bytes 65536 | tf_op jit(solution)/shard_map/all_to_all | solution.py:52
  15.1 2.6 all-to-all-done
  19.7 6.7 %gather_fusion = bf16[128,2,128,128]{3,2,1,0:T(8,128)(2,1)} fusion(bf16[2,2,128,4,128]{4,2,3,1,0:T(8,128)(2,1)S(1)} %pad_maximum_fusion.3, s32[128]{0:T(128)S(1)} %fusion.69), kind=kCustom, calls=%fused_computation | custom fusion | bytes 16778240 | tf_op jit(solution)/shard_map/gather | solution.py:64
  26.4 10.5 %all-to-all-start.1 = ((bf16[64,2,2,128,128]{4,3,2,1,0:T(8,128)(2,1)}), bf16[64,2,2,128,128]{4,3,2,1,0:T(8,128)(2,1)}, u32[]{:S(2)}, u32[]{:S(2)}) async-start(bf16[64,2,2,128,128]{4,3,2,1,0:T(8,128)(2,1)} %bitcast.311), calls=%async_computation.1 | async-start | bytes 16777216 | tf_op jit(solution)/shard_map/all_to_all | solution.py:65
  39.1 3.2 collective-permute-start.3
  48.1 2.9 collective-permute-start.5
  51.0 1.8 fusion.79
  52.8 188.3 %collective-permute-done.1 = bf16[2,256,512]{2,1,0:T(8,128)(2,1)} collective-permute-done((bf16[2,256,512]{2,1,0:T(8,128)(2,1)}, bf16[2,256,512]{2,1,0:T(8,128)(2,1)}, u32[]{:S(2)}, u32[]{:S(2)}) %collective-permute-start.1) | collective-permute-done | bytes 524320 | tf_op jit(solution)/shard_map/ppermute | solution.py:13
  241.1 1.9 fusion.78
  245.9 12.8 %collective-permute-done.3 = bf16[2,256,512]{2,1,0:T(8,128)(2,1)} collective-permute-done((bf16[2,256,512]{2,1,0:T(8,128)(2,1)}, bf16[2,256,512]{2,1,0:T(8,128)(2,1)}, u32[]{:S(2)}, u32[]{:S(2)}) %collective-permute-start.3) | collective-permute-done | bytes 524320 | tf_op jit(solution)/shard_map/ppermute | solution.py:13
  258.7 1.9 fusion.76
  262.2 1.8 fusion.75
  265.8 1.9 fusion.74
  271.1 1.8 copy.186
  274.6 1.8 copy.187
  278.1 1.8 copy.188
  281.6 1.8 copy.189
  285.2 1.8 copy.190
  288.7 1.8 copy.191
  297.8 2.7 bitcast_reduce_fusion
  300.5 5.3 gather_fusion.1
  314.6 6.4 %gather_fusion.2 = bf16[128,2,128,128]{3,2,1,0:T(8,128)(2,1)} fusion(bf16[25,2,128,128]{3,2,0,1:T(8,128)(2,1)S(1)} %concatenate.16, s32[1024]{0:T(1024)S(1)} %pad_clamp_fusion), kind=kCustom, calls=%fused_computation.2 | custom fusion | bytes 16777728 | tf_op jit(solution)/shard_map/gather | solution.py:130
  320.9 15.5 %all-to-all-start.2 = ((bf16[64,2,2,128,128]{4,3,2,1,0:T(8,128)(2,1)}), bf16[64,2,2,128,128]{4,3,2,1,0:T(8,128)(2,1)}, u32[]{:S(2)}, u32[]{:S(2)}) async-start(bf16[64,2,2,128,128]{4,3,2,1,0:T(8,128)(2,1)} %bitcast.310), calls=%async_computation.2 | async-start | bytes 16777216 | tf_op jit(solution)/shard_map/all_to_all | solution.py:132
  336.6 4.3 fusion.4
  347.0 1.8 fusion.32
  348.8 3.1 collective-permute-start.11
  355.1 2.4 collective-permute-start.8
  359.8 13.3 %collective-permute-done.11 = bf16[2,4,2,128,128]{4,3,2,1,0:T(8,128)(2,1)S(1)} collective-permute-done((bf16[2,4,2,128,128]{4,3,2,1,0:T(8,128)(2,1)}, bf16[2,4,2,128,128]{4,3,2,1,0:T(8,128)(2,1)S(1)}, u32[]{:S(2)}, u32[]{:S(2)}) %collective-permute-start.11) | collective-permute-done | bytes 524320 | tf_op jit(solution)/shard_map/ppermute | solution.py:13
  373.1 178.7 %all-to-all-done.2 = bf16[64,2,2,128,128]{4,3,2,1,0:T(8,128)(2,1)} async-done(((bf16[64,2,2,128,128]{4,3,2,1,0:T(8,128)(2,1)}), bf16[64,2,2,128,128]{4,3,2,1,0:T(8,128)(2,1)}, u32[]{:S(2)}, u32[]{:S(2)}) %all-to-all-start.2) | async-done | bytes 8388640 | tf_op jit(solution)/shard_map/all_to_all | solution.py:132
  551.8 8.2 %fusion.1 = f32[4,2,2,128,128]{4,0,3,2,1:T(4,128)S(1)} fusion(bf16[128,2,128,128]{3,2,1,0:T(8,128)(2,1)} %bitcast.91, s32[4,2]{0,1:T(2,128)S(1)} %multiply_add_fusion, s32[128]{0:T(128)S(1)} %eq.62), kind=kOutput, calls=%fused_computation.7 | convolution fusion | flops 67109888 | bytes 9437728 | tf_op jit(solution)/shard_map/tp,pksd->tksd/dot_general | solution.py:161
  560.0 3.2 collective-permute-done.8
  563.2 1.9 fusion.31
  (161 shorter events, 61.4 us)
Async XLA Ops:
  2.7 15.0 %all-to-all-start = ((s32[64,1,2]{2,1,0:T(1,128)}), s32[64,1,2]{2,1,0:T(1,128)S(1)}, u32[]{:S(2)}, u32[]{:S(2)}) async-start(s32[64,1,2]{2,1,0:T(1,128)} %bitcast.22), calls=%async_computation | async-start | bytes 65536 | tf_op jit(solution)/shard_map/all_to_all | solution.py:52
  26.4 10.5 %copy-start.14 = (bf16[256,512]{1,0:T(8,128)(2,1)S(1)}, bf16[256,512]{1,0:T(8,128)(2,1)}, u32[]{:S(2)}) copy-start(bf16[256,512]{1,0:T(8,128)(2,1)} %param.6) | copy-start | bytes 786436
  26.4 10.5 %copy-start.15 = (bf16[256,512]{1,0:T(8,128)(2,1)S(1)}, bf16[256,512]{1,0:T(8,128)(2,1)}, u32[]{:S(2)}) copy-start(bf16[256,512]{1,0:T(8,128)(2,1)} %param.7) | copy-start | bytes 786436
  26.4 274.0 %all-to-all-start.1 = ((bf16[64,2,2,128,128]{4,3,2,1,0:T(8,128)(2,1)}), bf16[64,2,2,128,128]{4,3,2,1,0:T(8,128)(2,1)}, u32[]{:S(2)}, u32[]{:S(2)}) async-start(bf16[64,2,2,128,128]{4,3,2,1,0:T(8,128)(2,1)} %bitcast.311), calls=%async_computation.1 | async-start | bytes 16777216 | tf_op jit(solution)/shard_map/all_to_all | solution.py:65
  37.8 8.2 %copy-start.26 = (bf16[256,512]{1,0:T(8,128)(2,1)S(1)}, bf16[256,512]{1,0:T(8,128)(2,1)}, u32[]{:S(2)}) copy-start(bf16[256,512]{1,0:T(8,128)(2,1)} %param.5) | copy-start | bytes 786436
  37.8 10.3 %collective-permute-start = (bf16[2,256,512]{2,1,0:T(8,128)(2,1)}, bf16[2,256,512]{2,1,0:T(8,128)(2,1)}, u32[]{:S(2)}, u32[]{:S(2)}) collective-permute-start(bf16[2,256,512]{2,1,0:T(8,128)(2,1)} %pad_maximum_fusion.2), channel_id=1, source_target_pairs={{0,4},{4,0},{8,12},{12,8},{16,20},{20,16},{24,28},{28,24},{32,36},... | collective-permute-start | bytes 1572872 | tf_op jit(solution)/shard_map/ppermute | solution.py:13
  37.9 203.1 %collective-permute-start.1 = (bf16[2,256,512]{2,1,0:T(8,128)(2,1)}, bf16[2,256,512]{2,1,0:T(8,128)(2,1)}, u32[]{:S(2)}, u32[]{:S(2)}) collective-permute-start(bf16[2,256,512]{2,1,0:T(8,128)(2,1)} %pad_maximum_fusion.2), channel_id=1, source_target_pairs={{0,8},{4,12},{8,0},{12,4},{16,24},{20,28},{24,16},{28,20},{32,40},... | collective-permute-start | bytes 1572872 | tf_op jit(solution)/shard_map/ppermute | solution.py:13
  38.5 204.4 %collective-permute-start.2 = (bf16[2,256,512]{2,1,0:T(8,128)(2,1)}, bf16[2,256,512]{2,1,0:T(8,128)(2,1)S(1)}, u32[]{:S(2)}, u32[]{:S(2)}) collective-permute-start(bf16[2,256,512]{2,1,0:T(8,128)(2,1)} %pad_maximum_fusion.2), channel_id=1, source_target_pairs={{0,16},{4,20},{8,24},{12,28},{16,0},{20,4},{24,8},{28,12},{32,48},... | collective-permute-start | bytes 1572872 | tf_op jit(solution)/shard_map/ppermute | solution.py:13
  39.1 219.6 %collective-permute-start.3 = (bf16[2,256,512]{2,1,0:T(8,128)(2,1)}, bf16[2,256,512]{2,1,0:T(8,128)(2,1)}, u32[]{:S(2)}, u32[]{:S(2)}) collective-permute-start(bf16[2,256,512]{2,1,0:T(8,128)(2,1)} %pad_maximum_fusion.2), channel_id=1, source_target_pairs={{0,32},{4,36},{8,40},{12,44},{16,48},{20,52},{24,56},{28,60},{32,0... | collective-permute-start | bytes 1572872 | tf_op jit(solution)/shard_map/ppermute | solution.py:13
  42.3 219.9 %collective-permute-start.4 = (bf16[2,256,512]{2,1,0:T(8,128)(2,1)}, bf16[2,256,512]{2,1,0:T(8,128)(2,1)}, u32[]{:S(2)}, u32[]{:S(2)}) collective-permute-start(bf16[2,256,512]{2,1,0:T(8,128)(2,1)} %pad_maximum_fusion.2), channel_id=1, source_target_pairs={{0,64},{4,68},{8,72},{12,76},{16,80},{20,84},{24,88},{28,92},{32,9... | collective-permute-start | bytes 1572872 | tf_op jit(solution)/shard_map/ppermute | solution.py:13
  46.1 267.4 %copy-start.12 = (bf16[2,128,4,128]{3,2,1,0:T(4,128)(2,1)}, bf16[2,128,4,128]{3,2,1,0:T(4,128)(2,1)S(1)}, u32[]{:S(2)}) copy-start(bf16[2,128,4,128]{3,2,1,0:T(4,128)(2,1)S(1)} %reshape.397) | copy-start | bytes 786436
  48.1 217.7 %collective-permute-start.5 = (bf16[2,256,512]{2,1,0:T(8,128)(2,1)}, bf16[2,256,512]{2,1,0:T(8,128)(2,1)}, u32[]{:S(2)}, u32[]{:S(2)}) collective-permute-start(bf16[2,256,512]{2,1,0:T(8,128)(2,1)} %pad_maximum_fusion.2), channel_id=1, source_target_pairs={{0,128},{4,132},{8,136},{12,140},{16,144},{20,148},{24,152},{28,15... | collective-permute-start | bytes 1572872 | tf_op jit(solution)/shard_map/ppermute | solution.py:13
  290.5 4.2 copy-start.16
  290.5 4.9 copy-start.17
  290.5 5.7 %copy-start.18 = (bf16[2,128,4,128]{1,3,0,2:T(8,128)(2,1)S(1)}, bf16[2,128,4,128]{1,3,0,2:T(8,128)(2,1)}, u32[]{:S(2)}) copy-start(bf16[2,128,4,128]{1,3,0,2:T(8,128)(2,1)} %copy.186) | copy-start | bytes 786436
  290.5 5.8 %copy-start.19 = (bf16[2,128,4,128]{1,3,0,2:T(8,128)(2,1)S(1)}, bf16[2,128,4,128]{1,3,0,2:T(8,128)(2,1)}, u32[]{:S(2)}) copy-start(bf16[2,128,4,128]{1,3,0,2:T(8,128)(2,1)} %copy.187) | copy-start | bytes 786436
  290.5 5.8 %copy-start.20 = (bf16[2,128,4,128]{1,3,0,2:T(8,128)(2,1)S(1)}, bf16[2,128,4,128]{1,3,0,2:T(8,128)(2,1)}, u32[]{:S(2)}) copy-start(bf16[2,128,4,128]{1,3,0,2:T(8,128)(2,1)} %copy.188) | copy-start | bytes 786436
  291.3 5.1 copy-start.21
  292.1 4.3 copy-start.22
  292.9 3.6 copy-start.23
  320.9 230.9 %all-to-all-start.2 = ((bf16[64,2,2,128,128]{4,3,2,1,0:T(8,128)(2,1)}), bf16[64,2,2,128,128]{4,3,2,1,0:T(8,128)(2,1)}, u32[]{:S(2)}, u32[]{:S(2)}) async-start(bf16[64,2,2,128,128]{4,3,2,1,0:T(8,128)(2,1)} %bitcast.310), calls=%async_computation.2 | async-start | bytes 16777216 | tf_op jit(solution)/shard_map/all_to_all | solution.py:132
  336.6 4.3 copy-start.13
  347.0 4.9 copy-start.9
  348.8 3.9 copy-start.11
  348.8 24.3 %collective-permute-start.11 = (bf16[2,4,2,128,128]{4,3,2,1,0:T(8,128)(2,1)}, bf16[2,4,2,128,128]{4,3,2,1,0:T(8,128)(2,1)S(1)}, u32[]{:S(2)}, u32[]{:S(2)}) collective-permute-start(bf16[2,4,2,128,128]{4,3,2,1,0:T(8,128)(2,1)} %get-tuple-element.14), channel_id=1, source_target_pairs={{0,128},{4,132},{8,136},{12,140},{16,144},{20,148},{24,152},{28,15... | collective-permute-start | bytes 1572872 | tf_op jit(solution)/shard_map/ppermute | solution.py:13
  353.8 206.2 %collective-permute-start.10 = (bf16[2,4,2,128,128]{4,3,2,1,0:T(8,128)(2,1)}, bf16[2,4,2,128,128]{4,3,2,1,0:T(8,128)(2,1)S(1)}, u32[]{:S(2)}, u32[]{:S(2)}) collective-permute-start(bf16[2,4,2,128,128]{4,3,2,1,0:T(8,128)(2,1)} %get-tuple-element.15), channel_id=1, source_target_pairs={{0,64},{4,68},{8,72},{12,76},{16,80},{20,84},{24,88},{28,92},{32,9... | collective-permute-start | bytes 1572872 | tf_op jit(solution)/shard_map/ppermute | solution.py:13
  354.6 205.4 %collective-permute-start.9 = (bf16[2,4,2,128,128]{4,3,2,1,0:T(8,128)(2,1)}, bf16[2,4,2,128,128]{4,3,2,1,0:T(8,128)(2,1)S(1)}, u32[]{:S(2)}, u32[]{:S(2)}) collective-permute-start(bf16[2,4,2,128,128]{4,3,2,1,0:T(8,128)(2,1)} %get-tuple-element.10), channel_id=1, source_target_pairs={{0,32},{4,36},{8,40},{12,44},{16,48},{20,52},{24,56},{28,60},{32,0... | collective-permute-start | bytes 1572872 | tf_op jit(solution)/shard_map/ppermute | solution.py:13
  355.1 208.1 %collective-permute-start.8 = (bf16[2,4,2,128,128]{4,3,2,1,0:T(8,128)(2,1)}, bf16[2,4,2,128,128]{4,3,2,1,0:T(8,128)(2,1)}, u32[]{:S(2)}, u32[]{:S(2)}) collective-permute-start(bf16[2,4,2,128,128]{4,3,2,1,0:T(8,128)(2,1)} %get-tuple-element.11), channel_id=1, source_target_pairs={{0,16},{4,20},{8,24},{12,28},{16,0},{20,4},{24,8},{28,12},{32,48},... | collective-permute-start | bytes 1572872 | tf_op jit(solution)/shard_map/ppermute | solution.py:13
  357.5 205.7 %collective-permute-start.7 = (bf16[2,4,2,128,128]{4,3,2,1,0:T(8,128)(2,1)}, bf16[2,4,2,128,128]{4,3,2,1,0:T(8,128)(2,1)}, u32[]{:S(2)}, u32[]{:S(2)}) collective-permute-start(bf16[2,4,2,128,128]{4,3,2,1,0:T(8,128)(2,1)} %get-tuple-element.12), channel_id=1, source_target_pairs={{0,8},{4,12},{8,0},{12,4},{16,24},{20,28},{24,16},{28,20},{32,40},... | collective-permute-start | bytes 1572872 | tf_op jit(solution)/shard_map/ppermute | solution.py:13
  373.1 190.1 %collective-permute-start.6 = (bf16[2,4,2,128,128]{4,3,2,1,0:T(8,128)(2,1)}, bf16[2,4,2,128,128]{4,3,2,1,0:T(8,128)(2,1)S(1)}, u32[]{:S(2)}, u32[]{:S(2)}) collective-permute-start(bf16[2,4,2,128,128]{4,3,2,1,0:T(8,128)(2,1)} %get-tuple-element.13), channel_id=1, source_target_pairs={{0,4},{4,0},{8,12},{12,8},{16,20},{20,16},{24,28},{28,24},{32,36},... | collective-permute-start | bytes 1572872 | tf_op jit(solution)/shard_map/ppermute | solution.py:13
  551.8 11.4 %copy-start.3 = (f32[1,4,2,8,128,128]{5,4,3,2,1,0:T(8,128)S(1)}, f32[1,4,2,8,128,128]{5,4,3,2,1,0:T(8,128)}, u32[]{:S(2)}) copy-start(f32[1,4,2,8,128,128]{5,4,3,2,1,0:T(8,128)} %copy-done.2) | copy-start | bytes 12582916
  551.8 11.4 %copy-start.5 = (f32[1,4,2,8,128,128]{5,4,3,2,1,0:T(8,128)S(1)}, f32[1,4,2,8,128,128]{5,4,3,2,1,0:T(8,128)}, u32[]{:S(2)}) copy-start(f32[1,4,2,8,128,128]{5,4,3,2,1,0:T(8,128)} %copy-done.4) | copy-start | bytes 12582916
  (10 other events, 17.5 us)
where the time goes:
time: 571 us; the launch traced here: 566 us
  waiting for transfers between devices  399 us (70%)
  local copies, waits for them, and re-layouts  83.4 us (15%)
  starting transfers between devices  53.4 us (9%)
  matrix products  21.7 us (4%)
  other arithmetic  7.91 us (1%)
    ppermute x12, waiting for transfers between devices, swapped(): return lax.ppermute(value, axis, pairs)  218 us
    all_to_all x1, waiting for transfers between devices, body(): lax.all_to_all(with_layout_constraint(send_terms.reshape(seq_devices, slo...  179 us
    another operation x22, local copies, waits for them, and re-layouts, heads_first(): arr.reshape(blk_count, blk_size, heads_here, head_size)  28.8 us
    ppermute x12, starting transfers between devices, swapped(): return lax.ppermute(value, axis, pairs)  17.2 us
    all_to_all x1, starting transfers between devices, body(): lax.all_to_all(with_layout_constraint(send_terms.reshape(seq_devices, slo...  15.5 us
    unnamed x69, local copies, waits for them, and re-layouts  14.8 us
  transfers between devices with their start and end apart: 15, of which 6 were waited for; matrix products, arithmetic and copies ran while one was open for 13% of the time, Pallas kernels for 0%

commit v1 on v0

--- a/solution.py
+++ b/solution.py
@@ -55,7 +55,9 @@
     asked_flat = asked_ids.reshape(-1)
 
     kv_rows = jnp.stack([keys, values])
-    far_kv = [swapped(kv_rows, "seq", far_level) for far_level in range(far_count)]
+    far_kv = []
+    for far_level in range(far_count):
+        far_kv.append(swapped(kv_rows, "seq", far_level))
 
     kv_four = kv_rows.reshape(2, blk_count, blk_size, heads_here, head_size)
     safe_ids = jnp.maximum(asked_flat, 0)
@@ -151,7 +153,8 @@
 
     grad_kv = terms[:, :, :, 0] + low(terms[:, :, :, 1])[:, :, ::-1]
     far_low = terms[:, :, :, 2:].astype(jnp.bfloat16)
-    for far_level in range(far_count):
+    slow_first = [0, 1, 4, 5, 3, 2] if far_count == 6 else list(range(far_count))
+    for far_level in slow_first:
         back = swapped(far_low[:, :, :, far_level], "seq", far_level)
         grad_kv = grad_kv + back.astype(f32)
     grad_rows = grad_kv.transpose(0, 2, 3, 1, 4)

time: 571 us -> 580 us (1.016)
  waiting for transfers between devices: 399 us -> 407 us
    ppermute x12, waiting for transfers between devices: 218 us -> 404 us  [swapped(): return lax.ppermute(value, axis, pairs)]
    all_to_all x1, waiting for transfers between devices: 179 us -> 0.01 us  [body(): lax.all_to_all(with_layout_constraint(send_terms.reshape(seq_devices, slo...]
  transfers between devices with their start and end apart: 15 -> 15, of which waited for: 6 -> 4; matrix products, arithmetic and copies ran while one was open for 13% -> 13% of each run, Pallas kernels for 0% -> 0%
where the time goes in v1:
time: 580 us; the launch traced here: 574 us
  waiting for transfers between devices  407 us (70%)
  local copies, waits for them, and re-layouts  83.8 us (14%)
  starting transfers between devices  53 us (9%)
  matrix products  21.7 us (4%)
  other arithmetic  7.91 us (1%)
    ppermute x12, waiting for transfers between devices, swapped(): return lax.ppermute(value, axis, pairs)  404 us
    another operation x22, local copies, waits for them, and re-layouts, heads_first(): arr.reshape(blk_count, blk_size, heads_here, head_size)  28.8 us
    ppermute x12, starting transfers between devices, swapped(): return lax.ppermute(value, axis, pairs)  16.8 us
    all_to_all x1, starting transfers between devices, body(): lax.all_to_all(with_layout_constraint(send_terms.reshape(seq_devices, slo...  15.5 us
    unnamed x69, local copies, waits for them, and re-layouts  15.2 us
  transfers between devices with their start and end apart: 15, of which 4 were waited for; matrix products, arithmetic and copies ran while one was open for 13% of the time, Pallas kernels for 0%

profile of v1, /device:TPU:152, one launch (start us, length us, event | category | flops | bytes accessed | tf_op | source)
XLA Modules:
  0.0 574.2 jit_solution(15152237632643733789)
XLA Ops:
  2.7 10.2 %all-to-all-start = ((s32[64,1,2]{2,1,0:T(1,128)}), s32[64,1,2]{2,1,0:T(1,128)S(1)}, u32[]{:S(2)}, u32[]{:S(2)}) async-start(s32[64,1,2]{2,1,0:T(1,128)} %bitcast.22), calls=%async_computation | async-start | bytes 65536 | tf_op jit(solution)/shard_map/all_to_all | solution.py:52
  15.1 2.6 all-to-all-done
  19.7 6.7 %gather_fusion = bf16[128,2,128,128]{3,2,1,0:T(8,128)(2,1)} fusion(bf16[2,2,128,4,128]{4,2,3,1,0:T(8,128)(2,1)S(1)} %pad_maximum_fusion.3, s32[128]{0:T(128)S(1)} %fusion.69), kind=kCustom, calls=%fused_computation | custom fusion | bytes 16778240 | tf_op jit(solution)/shard_map/gather | solution.py:66
  26.4 10.5 %all-to-all-start.1 = ((bf16[64,2,2,128,128]{4,3,2,1,0:T(8,128)(2,1)}), bf16[64,2,2,128,128]{4,3,2,1,0:T(8,128)(2,1)}, u32[]{:S(2)}, u32[]{:S(2)}) async-start(bf16[64,2,2,128,128]{4,3,2,1,0:T(8,128)(2,1)} %bitcast.311), calls=%async_computation.1 | async-start | bytes 16777216 | tf_op jit(solution)/shard_map/all_to_all | solution.py:67
  39.1 3.2 collective-permute-start.3
  48.1 2.9 collective-permute-start.5
  51.0 1.8 fusion.79
  52.8 188.3 %collective-permute-done.1 = bf16[2,256,512]{2,1,0:T(8,128)(2,1)} collective-permute-done((bf16[2,256,512]{2,1,0:T(8,128)(2,1)}, bf16[2,256,512]{2,1,0:T(8,128)(2,1)}, u32[]{:S(2)}, u32[]{:S(2)}) %collective-permute-start.1) | collective-permute-done | bytes 524320 | tf_op jit(solution)/shard_map/ppermute | solution.py:13
  241.1 1.9 fusion.78
  245.9 12.8 %collective-permute-done.3 = bf16[2,256,512]{2,1,0:T(8,128)(2,1)} collective-permute-done((bf16[2,256,512]{2,1,0:T(8,128)(2,1)}, bf16[2,256,512]{2,1,0:T(8,128)(2,1)}, u32[]{:S(2)}, u32[]{:S(2)}) %collective-permute-start.3) | collective-permute-done | bytes 524320 | tf_op jit(solution)/shard_map/ppermute | solution.py:13
  258.7 1.9 fusion.76
  260.5 1.7 reshape_squeeze.39
  262.2 1.8 fusion.75
  265.8 1.9 fusion.74
  271.1 1.8 copy.186
  274.6 1.8 copy.187
  278.1 1.8 copy.188
  281.6 1.8 copy.189
  285.2 1.8 copy.190
  288.7 1.8 copy.191
  292.9 1.7 bitcast_dynamic-update-slice_fusion.9
  297.8 2.7 bitcast_reduce_fusion
  300.5 5.3 gather_fusion.1
  314.6 6.4 %gather_fusion.2 = bf16[128,2,128,128]{3,2,1,0:T(8,128)(2,1)} fusion(bf16[25,2,128,128]{3,2,0,1:T(8,128)(2,1)S(1)} %concatenate.16, s32[1024]{0:T(1024)S(1)} %pad_clamp_fusion), kind=kCustom, calls=%fused_computation.2 | custom fusion | bytes 16777728 | tf_op jit(solution)/shard_map/gather | solution.py:132
  320.9 15.5 %all-to-all-start.2 = ((bf16[64,2,2,128,128]{4,3,2,1,0:T(8,128)(2,1)}), bf16[64,2,2,128,128]{4,3,2,1,0:T(8,128)(2,1)}, u32[]{:S(2)}, u32[]{:S(2)}) async-start(bf16[64,2,2,128,128]{4,3,2,1,0:T(8,128)(2,1)} %bitcast.310), calls=%async_computation.2 | async-start | bytes 16777216 | tf_op jit(solution)/shard_map/all_to_all | solution.py:134
  336.6 4.3 fusion.4
  347.0 1.8 fusion.32
  351.7 2.0 collective-permute-start.10
  353.7 3.1 collective-permute-start.9
  359.8 202.9 %collective-permute-done.11 = bf16[2,4,2,128,128]{4,3,2,1,0:T(8,128)(2,1)S(1)} collective-permute-done((bf16[2,4,2,128,128]{4,3,2,1,0:T(8,128)(2,1)}, bf16[2,4,2,128,128]{4,3,2,1,0:T(8,128)(2,1)S(1)}, u32[]{:S(2)}, u32[]{:S(2)}) %collective-permute-start.11) | collective-permute-done | bytes 524320 | tf_op jit(solution)/shard_map/ppermute | solution.py:13
  562.7 8.2 %fusion.1 = f32[4,2,2,128,128]{4,0,3,2,1:T(4,128)S(1)} fusion(bf16[128,2,128,128]{3,2,1,0:T(8,128)(2,1)} %bitcast.91, s32[4,2]{0,1:T(2,128)S(1)} %multiply_add_fusion, s32[128]{0:T(128)S(1)} %eq.62), kind=kOutput, calls=%fused_computation.7 | convolution fusion | flops 67109888 | bytes 9437728 | tf_op jit(solution)/shard_map/tp,pksd->tksd/dot_general | solution.py:164
  571.0 1.9 fusion.31
  (161 shorter events, 58.3 us)
Async XLA Ops:
  2.7 15.0 %all-to-all-start = ((s32[64,1,2]{2,1,0:T(1,128)}), s32[64,1,2]{2,1,0:T(1,128)S(1)}, u32[]{:S(2)}, u32[]{:S(2)}) async-start(s32[64,1,2]{2,1,0:T(1,128)} %bitcast.22), calls=%async_computation | async-start | bytes 65536 | tf_op jit(solution)/shard_map/all_to_all | solution.py:52
  26.4 10.5 %copy-start.14 = (bf16[256,512]{1,0:T(8,128)(2,1)S(1)}, bf16[256,512]{1,0:T(8,128)(2,1)}, u32[]{:S(2)}) copy-start(bf16[256,512]{1,0:T(8,128)(2,1)} %param.6) | copy-start | bytes 786436
  26.4 10.5 %copy-start.15 = (bf16[256,512]{1,0:T(8,128)(2,1)S(1)}, bf16[256,512]{1,0:T(8,128)(2,1)}, u32[]{:S(2)}) copy-start(bf16[256,512]{1,0:T(8,128)(2,1)} %param.7) | copy-start | bytes 786436
  26.4 274.0 %all-to-all-start.1 = ((bf16[64,2,2,128,128]{4,3,2,1,0:T(8,128)(2,1)}), bf16[64,2,2,128,128]{4,3,2,1,0:T(8,128)(2,1)}, u32[]{:S(2)}, u32[]{:S(2)}) async-start(bf16[64,2,2,128,128]{4,3,2,1,0:T(8,128)(2,1)} %bitcast.311), calls=%async_computation.1 | async-start | bytes 16777216 | tf_op jit(solution)/shard_map/all_to_all | solution.py:67
  37.8 8.2 %copy-start.26 = (bf16[256,512]{1,0:T(8,128)(2,1)S(1)}, bf16[256,512]{1,0:T(8,128)(2,1)}, u32[]{:S(2)}) copy-start(bf16[256,512]{1,0:T(8,128)(2,1)} %param.5) | copy-start | bytes 786436
  37.8 10.3 %collective-permute-start = (bf16[2,256,512]{2,1,0:T(8,128)(2,1)}, bf16[2,256,512]{2,1,0:T(8,128)(2,1)}, u32[]{:S(2)}, u32[]{:S(2)}) collective-permute-start(bf16[2,256,512]{2,1,0:T(8,128)(2,1)} %pad_maximum_fusion.2), channel_id=1, source_target_pairs={{0,4},{4,0},{8,12},{12,8},{16,20},{20,16},{24,28},{28,24},{32,36},... | collective-permute-start | bytes 1572872 | tf_op jit(solution)/shard_map/ppermute | solution.py:13
  37.9 203.1 %collective-permute-start.1 = (bf16[2,256,512]{2,1,0:T(8,128)(2,1)}, bf16[2,256,512]{2,1,0:T(8,128)(2,1)}, u32[]{:S(2)}, u32[]{:S(2)}) collective-permute-start(bf16[2,256,512]{2,1,0:T(8,128)(2,1)} %pad_maximum_fusion.2), channel_id=1, source_target_pairs={{0,8},{4,12},{8,0},{12,4},{16,24},{20,28},{24,16},{28,20},{32,40},... | collective-permute-start | bytes 1572872 | tf_op jit(solution)/shard_map/ppermute | solution.py:13
  38.5 204.4 %collective-permute-start.2 = (bf16[2,256,512]{2,1,0:T(8,128)(2,1)}, bf16[2,256,512]{2,1,0:T(8,128)(2,1)S(1)}, u32[]{:S(2)}, u32[]{:S(2)}) collective-permute-start(bf16[2,256,512]{2,1,0:T(8,128)(2,1)} %pad_maximum_fusion.2), channel_id=1, source_target_pairs={{0,16},{4,20},{8,24},{12,28},{16,0},{20,4},{24,8},{28,12},{32,48},... | collective-permute-start | bytes 1572872 | tf_op jit(solution)/shard_map/ppermute | solution.py:13
  39.1 219.6 %collective-permute-start.3 = (bf16[2,256,512]{2,1,0:T(8,128)(2,1)}, bf16[2,256,512]{2,1,0:T(8,128)(2,1)}, u32[]{:S(2)}, u32[]{:S(2)}) collective-permute-start(bf16[2,256,512]{2,1,0:T(8,128)(2,1)} %pad_maximum_fusion.2), channel_id=1, source_target_pairs={{0,32},{4,36},{8,40},{12,44},{16,48},{20,52},{24,56},{28,60},{32,0... | collective-permute-start | bytes 1572872 | tf_op jit(solution)/shard_map/ppermute | solution.py:13
  42.3 219.9 %collective-permute-start.4 = (bf16[2,256,512]{2,1,0:T(8,128)(2,1)}, bf16[2,256,512]{2,1,0:T(8,128)(2,1)}, u32[]{:S(2)}, u32[]{:S(2)}) collective-permute-start(bf16[2,256,512]{2,1,0:T(8,128)(2,1)} %pad_maximum_fusion.2), channel_id=1, source_target_pairs={{0,64},{4,68},{8,72},{12,76},{16,80},{20,84},{24,88},{28,92},{32,9... | collective-permute-start | bytes 1572872 | tf_op jit(solution)/shard_map/ppermute | solution.py:13
  46.1 267.4 %copy-start.12 = (bf16[2,128,4,128]{3,2,1,0:T(4,128)(2,1)}, bf16[2,128,4,128]{3,2,1,0:T(4,128)(2,1)S(1)}, u32[]{:S(2)}) copy-start(bf16[2,128,4,128]{3,2,1,0:T(4,128)(2,1)S(1)} %reshape.397) | copy-start | bytes 786436
  48.1 217.7 %collective-permute-start.5 = (bf16[2,256,512]{2,1,0:T(8,128)(2,1)}, bf16[2,256,512]{2,1,0:T(8,128)(2,1)}, u32[]{:S(2)}, u32[]{:S(2)}) collective-permute-start(bf16[2,256,512]{2,1,0:T(8,128)(2,1)} %pad_maximum_fusion.2), channel_id=1, source_target_pairs={{0,128},{4,132},{8,136},{12,140},{16,144},{20,148},{24,152},{28,15... | collective-permute-start | bytes 1572872 | tf_op jit(solution)/shard_map/ppermute | solution.py:13
  290.5 4.2 copy-start.16
  290.5 4.9 copy-start.17
  290.5 5.7 copy-start.18
  290.5 5.8 %copy-start.19 = (bf16[2,128,4,128]{1,3,0,2:T(8,128)(2,1)S(1)}, bf16[2,128,4,128]{1,3,0,2:T(8,128)(2,1)}, u32[]{:S(2)}) copy-start(bf16[2,128,4,128]{1,3,0,2:T(8,128)(2,1)} %copy.187) | copy-start | bytes 786436
  290.5 5.8 %copy-start.20 = (bf16[2,128,4,128]{1,3,0,2:T(8,128)(2,1)S(1)}, bf16[2,128,4,128]{1,3,0,2:T(8,128)(2,1)}, u32[]{:S(2)}) copy-start(bf16[2,128,4,128]{1,3,0,2:T(8,128)(2,1)} %copy.188) | copy-start | bytes 786436
  291.3 5.1 copy-start.21
  292.1 4.3 copy-start.22
  292.9 3.6 copy-start.23
  305.8 2.7 copy-start
  320.9 241.8 %all-to-all-start.2 = ((bf16[64,2,2,128,128]{4,3,2,1,0:T(8,128)(2,1)}), bf16[64,2,2,128,128]{4,3,2,1,0:T(8,128)(2,1)}, u32[]{:S(2)}, u32[]{:S(2)}) async-start(bf16[64,2,2,128,128]{4,3,2,1,0:T(8,128)(2,1)} %bitcast.310), calls=%async_computation.2 | async-start | bytes 16777216 | tf_op jit(solution)/shard_map/all_to_all | solution.py:134
  336.6 4.3 copy-start.13
  347.0 2.7 copy-start.9
  348.8 213.9 %collective-permute-start.11 = (bf16[2,4,2,128,128]{4,3,2,1,0:T(8,128)(2,1)}, bf16[2,4,2,128,128]{4,3,2,1,0:T(8,128)(2,1)S(1)}, u32[]{:S(2)}, u32[]{:S(2)}) collective-permute-start(bf16[2,4,2,128,128]{4,3,2,1,0:T(8,128)(2,1)} %get-tuple-element.14), channel_id=1, source_target_pairs={{0,16},{4,20},{8,24},{12,28},{16,0},{20,4},{24,8},{28,12},{32,48},... | collective-permute-start | bytes 1572872 | tf_op jit(solution)/shard_map/ppermute | solution.py:13
  351.7 219.2 %collective-permute-start.10 = (bf16[2,4,2,128,128]{4,3,2,1,0:T(8,128)(2,1)}, bf16[2,4,2,128,128]{4,3,2,1,0:T(8,128)(2,1)S(1)}, u32[]{:S(2)}, u32[]{:S(2)}) collective-permute-start(bf16[2,4,2,128,128]{4,3,2,1,0:T(8,128)(2,1)} %get-tuple-element.15), channel_id=1, source_target_pairs={{0,32},{4,36},{8,40},{12,44},{16,48},{20,52},{24,56},{28,60},{32,0... | collective-permute-start | bytes 1572872 | tf_op jit(solution)/shard_map/ppermute | solution.py:13
  353.7 217.2 %collective-permute-start.9 = (bf16[2,4,2,128,128]{4,3,2,1,0:T(8,128)(2,1)}, bf16[2,4,2,128,128]{4,3,2,1,0:T(8,128)(2,1)S(1)}, u32[]{:S(2)}, u32[]{:S(2)}) collective-permute-start(bf16[2,4,2,128,128]{4,3,2,1,0:T(8,128)(2,1)} %get-tuple-element.10), channel_id=1, source_target_pairs={{0,128},{4,132},{8,136},{12,140},{16,144},{20,148},{24,152},{28,15... | collective-permute-start | bytes 1572872 | tf_op jit(solution)/shard_map/ppermute | solution.py:13
  356.8 214.1 %collective-permute-start.8 = (bf16[2,4,2,128,128]{4,3,2,1,0:T(8,128)(2,1)}, bf16[2,4,2,128,128]{4,3,2,1,0:T(8,128)(2,1)}, u32[]{:S(2)}, u32[]{:S(2)}) collective-permute-start(bf16[2,4,2,128,128]{4,3,2,1,0:T(8,128)(2,1)} %get-tuple-element.11), channel_id=1, source_target_pairs={{0,64},{4,68},{8,72},{12,76},{16,80},{20,84},{24,88},{28,92},{32,9... | collective-permute-start | bytes 1572872 | tf_op jit(solution)/shard_map/ppermute | solution.py:13
  357.5 213.4 %collective-permute-start.7 = (bf16[2,4,2,128,128]{4,3,2,1,0:T(8,128)(2,1)}, bf16[2,4,2,128,128]{4,3,2,1,0:T(8,128)(2,1)}, u32[]{:S(2)}, u32[]{:S(2)}) collective-permute-start(bf16[2,4,2,128,128]{4,3,2,1,0:T(8,128)(2,1)} %get-tuple-element.12), channel_id=1, source_target_pairs={{0,8},{4,12},{8,0},{12,4},{16,24},{20,28},{24,16},{28,20},{32,40},... | collective-permute-start | bytes 1572872 | tf_op jit(solution)/shard_map/ppermute | solution.py:13
  562.7 8.2 %collective-permute-start.6 = (bf16[2,4,2,128,128]{4,3,2,1,0:T(8,128)(2,1)}, bf16[2,4,2,128,128]{4,3,2,1,0:T(8,128)(2,1)S(1)}, u32[]{:S(2)}, u32[]{:S(2)}) collective-permute-start(bf16[2,4,2,128,128]{4,3,2,1,0:T(8,128)(2,1)} %get-tuple-element.13), channel_id=1, source_target_pairs={{0,4},{4,0},{8,12},{12,8},{16,20},{20,16},{24,28},{28,24},{32,36},... | collective-permute-start | bytes 1572872 | tf_op jit(solution)/shard_map/ppermute | solution.py:13
  562.7 8.2 %copy-start.3 = (f32[1,4,2,8,128,128]{5,4,3,2,1,0:T(8,128)S(1)}, f32[1,4,2,8,128,128]{5,4,3,2,1,0:T(8,128)}, u32[]{:S(2)}) copy-start(f32[1,4,2,8,128,128]{5,4,3,2,1,0:T(8,128)} %copy-done.2) | copy-start | bytes 12582916
  562.7 8.3 %copy-start.5 = (f32[1,4,2,8,128,128]{5,4,3,2,1,0:T(8,128)S(1)}, f32[1,4,2,8,128,128]{5,4,3,2,1,0:T(8,128)}, u32[]{:S(2)}) copy-start(f32[1,4,2,8,128,128]{5,4,3,2,1,0:T(8,128)} %copy-done.4) | copy-start | bytes 12582916
  (10 other events, 16.5 us)

commit v2 on v0

--- a/solution.py
+++ b/solution.py
@@ -57,11 +57,13 @@
     kv_rows = jnp.stack([keys, values])
     far_kv = [swapped(kv_rows, "seq", far_level) for far_level in range(far_count)]
 
-    kv_four = kv_rows.reshape(2, blk_count, blk_size, heads_here, head_size)
+    kv_items = (
+        kv_rows.reshape(2, blk_count, blk_size, heads_here, head_size)
+        .transpose(3, 1, 0, 2, 4)
+        .reshape(heads_here * blk_count, 2, blk_size, head_size)
+    )
     safe_ids = jnp.maximum(asked_flat, 0)
-    pick_head = safe_ids // blk_count
-    pick_blk = safe_ids % blk_count
-    kv_pick = kv_four[:, pick_blk, :, pick_head, :]
+    kv_pick = kv_items[safe_ids]
     kv_back = lax.all_to_all(
         kv_pick.reshape(seq_devices, slot_cap, 2, blk_size, head_size),
         "seq",
@@ -151,7 +153,8 @@
 
     grad_kv = terms[:, :, :, 0] + low(terms[:, :, :, 1])[:, :, ::-1]
     far_low = terms[:, :, :, 2:].astype(jnp.bfloat16)
-    for far_level in range(far_count):
+    slow_first = [0, 1, 4, 5, 3, 2] if far_count == 6 else list(range(far_count))
+    for far_level in slow_first:
         back = swapped(far_low[:, :, :, far_level], "seq", far_level)
         grad_kv = grad_kv + back.astype(f32)
     grad_rows = grad_kv.transpose(0, 2, 3, 1, 4)

time: 571 us -> 579 us (1.014)
  waiting for transfers between devices: 399 us -> 406 us
    ppermute x12, waiting for transfers between devices: 218 us -> 404 us  [swapped(): return lax.ppermute(value, axis, pairs)]
    all_to_all x1, waiting for transfers between devices: 179 us -> 0.01 us  [body(): lax.all_to_all(with_layout_constraint(send_terms.reshape(seq_devices, slo...]
  transfers between devices with their start and end apart: 15 -> 15, of which waited for: 6 -> 4; matrix products, arithmetic and copies ran while one was open for 13% -> 13% of each run, Pallas kernels for 0% -> 0%
where the time goes in v2:
time: 579 us; the launch traced here: 573 us
  waiting for transfers between devices  406 us (70%)
  local copies, waits for them, and re-layouts  83.2 us (14%)
  starting transfers between devices  53 us (9%)
  matrix products  21.7 us (4%)
  other arithmetic  7.95 us (1%)
    ppermute x12, waiting for transfers between devices, swapped(): return lax.ppermute(value, axis, pairs)  404 us
    another operation x22, local copies, waits for them, and re-layouts, heads_first(): arr.reshape(blk_count, blk_size, heads_here, head_size)  28.8 us
    ppermute x12, starting transfers between devices, swapped(): return lax.ppermute(value, axis, pairs)  16.8 us
    all_to_all x1, starting transfers between devices, body(): lax.all_to_all(with_layout_constraint(send_terms.reshape(seq_devices, slo...  15.5 us
    unnamed x69, local copies, waits for them, and re-layouts  15.3 us
  transfers between devices with their start and end apart: 15, of which 4 were waited for; matrix products, arithmetic and copies ran while one was open for 13% of the time, Pallas kernels for 0%

profile of v2, /device:TPU:152, one launch (start us, length us, event | category | flops | bytes accessed | tf_op | source)
XLA Modules:
  0.0 573.1 jit_solution(3687045188234116987)
XLA Ops:
  2.7 10.2 %all-to-all-start = ((s32[64,1,2]{2,1,0:T(1,128)}), s32[64,1,2]{2,1,0:T(1,128)S(1)}, u32[]{:S(2)}, u32[]{:S(2)}) async-start(s32[64,1,2]{2,1,0:T(1,128)} %bitcast.24), calls=%async_computation | async-start | bytes 65536 | tf_op jit(solution)/shard_map/all_to_all | solution.py:52
  15.4 2.3 all-to-all-done
  19.2 6.2 %gather_fusion = bf16[128,2,128,128]{3,2,1,0:T(8,128)(2,1)} fusion(bf16[8,2,128,128]{3,2,1,0:T(8,128)(2,1)S(1)} %bitcast.311, s32[1024]{0:T(1024)S(1)} %pad_clamp_fusion.2), kind=kCustom, calls=%fused_computation | custom fusion | bytes 16777728 | tf_op jit(solution)/shard_map/gather | solution.py:66
  25.4 10.5 %all-to-all-start.1 = ((bf16[64,2,2,128,128]{4,3,2,1,0:T(8,128)(2,1)}), bf16[64,2,2,128,128]{4,3,2,1,0:T(8,128)(2,1)}, u32[]{:S(2)}, u32[]{:S(2)}) async-start(bf16[64,2,2,128,128]{4,3,2,1,0:T(8,128)(2,1)} %bitcast.312), calls=%async_computation.1 | async-start | bytes 16777216 | tf_op jit(solution)/shard_map/all_to_all | solution.py:67
  38.0 3.2 collective-permute-start.3
  47.2 2.9 collective-permute-start.5
  50.1 1.8 fusion.73
  51.8 188.2 %collective-permute-done.1 = bf16[2,256,512]{2,1,0:T(8,128)(2,1)} collective-permute-done((bf16[2,256,512]{2,1,0:T(8,128)(2,1)}, bf16[2,256,512]{2,1,0:T(8,128)(2,1)}, u32[]{:S(2)}, u32[]{:S(2)}) %collective-permute-start.1) | collective-permute-done | bytes 524320 | tf_op jit(solution)/shard_map/ppermute | solution.py:13
  240.0 1.9 fusion.72
  244.8 12.8 %collective-permute-done.3 = bf16[2,256,512]{2,1,0:T(8,128)(2,1)} collective-permute-done((bf16[2,256,512]{2,1,0:T(8,128)(2,1)}, bf16[2,256,512]{2,1,0:T(8,128)(2,1)}, u32[]{:S(2)}, u32[]{:S(2)}) %collective-permute-start.3) | collective-permute-done | bytes 524320 | tf_op jit(solution)/shard_map/ppermute | solution.py:13
  257.6 1.9 fusion.70
  261.2 1.9 fusion.69
  263.0 1.7 reshape_squeeze.40
  264.8 1.9 fusion.68
  270.1 1.8 copy.183
  273.6 1.8 copy.184
  277.1 1.8 copy.185
  280.7 1.8 copy.186
  284.2 1.8 copy.187
  287.7 1.8 copy.188
  291.9 1.8 bitcast_dynamic-update-slice_fusion.9
  296.8 2.7 bitcast_reduce_fusion
  299.4 5.3 gather_fusion.1
  313.5 6.4 %gather_fusion.2 = bf16[128,2,128,128]{3,2,1,0:T(8,128)(2,1)} fusion(bf16[25,2,128,128]{3,2,0,1:T(8,128)(2,1)S(1)} %concatenate.12, s32[1024]{0:T(1024)S(1)} %pad_clamp_fusion), kind=kCustom, calls=%fused_computation.2 | custom fusion | bytes 16777728 | tf_op jit(solution)/shard_map/gather | solution.py:132
  319.9 15.5 %all-to-all-start.2 = ((bf16[64,2,2,128,128]{4,3,2,1,0:T(8,128)(2,1)}), bf16[64,2,2,128,128]{4,3,2,1,0:T(8,128)(2,1)}, u32[]{:S(2)}, u32[]{:S(2)}) async-start(bf16[64,2,2,128,128]{4,3,2,1,0:T(8,128)(2,1)} %bitcast.313), calls=%async_computation.2 | async-start | bytes 16777216 | tf_op jit(solution)/shard_map/all_to_all | solution.py:134
  335.6 4.3 fusion.4
  346.0 1.8 fusion.32
  350.7 2.0 collective-permute-start.10
  352.7 3.1 collective-permute-start.9
  358.8 202.8 %collective-permute-done.11 = bf16[2,4,2,128,128]{4,3,2,1,0:T(8,128)(2,1)S(1)} collective-permute-done((bf16[2,4,2,128,128]{4,3,2,1,0:T(8,128)(2,1)}, bf16[2,4,2,128,128]{4,3,2,1,0:T(8,128)(2,1)S(1)}, u32[]{:S(2)}, u32[]{:S(2)}) %collective-permute-start.11) | collective-permute-done | bytes 524320 | tf_op jit(solution)/shard_map/ppermute | solution.py:13
  561.7 8.2 %fusion.1 = f32[4,2,2,128,128]{4,0,3,2,1:T(4,128)S(1)} fusion(bf16[128,2,128,128]{3,2,1,0:T(8,128)(2,1)} %bitcast.92, s32[4,2]{0,1:T(2,128)S(1)} %multiply_add_fusion, s32[128]{0:T(128)S(1)} %eq.60), kind=kOutput, calls=%fused_computation.7 | convolution fusion | flops 67109888 | bytes 9437728 | tf_op jit(solution)/shard_map/tp,pksd->tksd/dot_general | solution.py:164
  569.9 1.9 fusion.31
  (157 shorter events, 58.1 us)
Async XLA Ops:
  2.7 15.0 %all-to-all-start = ((s32[64,1,2]{2,1,0:T(1,128)}), s32[64,1,2]{2,1,0:T(1,128)S(1)}, u32[]{:S(2)}, u32[]{:S(2)}) async-start(s32[64,1,2]{2,1,0:T(1,128)} %bitcast.24), calls=%async_computation | async-start | bytes 65536 | tf_op jit(solution)/shard_map/all_to_all | solution.py:52
  25.4 10.5 %copy-start.14 = (bf16[256,512]{1,0:T(8,128)(2,1)S(1)}, bf16[256,512]{1,0:T(8,128)(2,1)}, u32[]{:S(2)}) copy-start(bf16[256,512]{1,0:T(8,128)(2,1)} %param.6) | copy-start | bytes 786436
  25.4 10.5 %copy-start.15 = (bf16[256,512]{1,0:T(8,128)(2,1)S(1)}, bf16[256,512]{1,0:T(8,128)(2,1)}, u32[]{:S(2)}) copy-start(bf16[256,512]{1,0:T(8,128)(2,1)} %param.7) | copy-start | bytes 786436
  25.4 274.0 %all-to-all-start.1 = ((bf16[64,2,2,128,128]{4,3,2,1,0:T(8,128)(2,1)}), bf16[64,2,2,128,128]{4,3,2,1,0:T(8,128)(2,1)}, u32[]{:S(2)}, u32[]{:S(2)}) async-start(bf16[64,2,2,128,128]{4,3,2,1,0:T(8,128)(2,1)} %bitcast.312), calls=%async_computation.1 | async-start | bytes 16777216 | tf_op jit(solution)/shard_map/all_to_all | solution.py:67
  36.8 8.3 %copy-start.26 = (bf16[256,512]{1,0:T(8,128)(2,1)S(1)}, bf16[256,512]{1,0:T(8,128)(2,1)}, u32[]{:S(2)}) copy-start(bf16[256,512]{1,0:T(8,128)(2,1)} %param.5) | copy-start | bytes 786436
  36.8 10.4 %collective-permute-start = (bf16[2,256,512]{2,1,0:T(8,128)(2,1)}, bf16[2,256,512]{2,1,0:T(8,128)(2,1)}, u32[]{:S(2)}, u32[]{:S(2)}) collective-permute-start(bf16[2,256,512]{2,1,0:T(8,128)(2,1)} %pad_maximum_fusion.2), channel_id=1, source_target_pairs={{0,4},{4,0},{8,12},{12,8},{16,20},{20,16},{24,28},{28,24},{32,36},... | collective-permute-start | bytes 1572872 | tf_op jit(solution)/shard_map/ppermute | solution.py:13
  36.9 203.1 %collective-permute-start.1 = (bf16[2,256,512]{2,1,0:T(8,128)(2,1)}, bf16[2,256,512]{2,1,0:T(8,128)(2,1)}, u32[]{:S(2)}, u32[]{:S(2)}) collective-permute-start(bf16[2,256,512]{2,1,0:T(8,128)(2,1)} %pad_maximum_fusion.2), channel_id=1, source_target_pairs={{0,8},{4,12},{8,0},{12,4},{16,24},{20,28},{24,16},{28,20},{32,40},... | collective-permute-start | bytes 1572872 | tf_op jit(solution)/shard_map/ppermute | solution.py:13
  37.5 204.4 %collective-permute-start.2 = (bf16[2,256,512]{2,1,0:T(8,128)(2,1)}, bf16[2,256,512]{2,1,0:T(8,128)(2,1)S(1)}, u32[]{:S(2)}, u32[]{:S(2)}) collective-permute-start(bf16[2,256,512]{2,1,0:T(8,128)(2,1)} %pad_maximum_fusion.2), channel_id=1, source_target_pairs={{0,16},{4,20},{8,24},{12,28},{16,0},{20,4},{24,8},{28,12},{32,48},... | collective-permute-start | bytes 1572872 | tf_op jit(solution)/shard_map/ppermute | solution.py:13
  38.0 219.6 %collective-permute-start.3 = (bf16[2,256,512]{2,1,0:T(8,128)(2,1)}, bf16[2,256,512]{2,1,0:T(8,128)(2,1)}, u32[]{:S(2)}, u32[]{:S(2)}) collective-permute-start(bf16[2,256,512]{2,1,0:T(8,128)(2,1)} %pad_maximum_fusion.2), channel_id=1, source_target_pairs={{0,32},{4,36},{8,40},{12,44},{16,48},{20,52},{24,56},{28,60},{32,0... | collective-permute-start | bytes 1572872 | tf_op jit(solution)/shard_map/ppermute | solution.py:13
  41.3 219.9 %collective-permute-start.4 = (bf16[2,256,512]{2,1,0:T(8,128)(2,1)}, bf16[2,256,512]{2,1,0:T(8,128)(2,1)}, u32[]{:S(2)}, u32[]{:S(2)}) collective-permute-start(bf16[2,256,512]{2,1,0:T(8,128)(2,1)} %pad_maximum_fusion.2), channel_id=1, source_target_pairs={{0,64},{4,68},{8,72},{12,76},{16,80},{20,84},{24,88},{28,92},{32,9... | collective-permute-start | bytes 1572872 | tf_op jit(solution)/shard_map/ppermute | solution.py:13
  45.1 267.3 %copy-start.12 = (bf16[2,128,4,128]{3,2,1,0:T(4,128)(2,1)}, bf16[2,128,4,128]{3,2,1,0:T(4,128)(2,1)S(1)}, u32[]{:S(2)}) copy-start(bf16[2,128,4,128]{3,2,1,0:T(4,128)(2,1)S(1)} %reshape.332) | copy-start | bytes 786436
  47.2 217.6 %collective-permute-start.5 = (bf16[2,256,512]{2,1,0:T(8,128)(2,1)}, bf16[2,256,512]{2,1,0:T(8,128)(2,1)}, u32[]{:S(2)}, u32[]{:S(2)}) collective-permute-start(bf16[2,256,512]{2,1,0:T(8,128)(2,1)} %pad_maximum_fusion.2), channel_id=1, source_target_pairs={{0,128},{4,132},{8,136},{12,140},{16,144},{20,148},{24,152},{28,15... | collective-permute-start | bytes 1572872 | tf_op jit(solution)/shard_map/ppermute | solution.py:13
  289.5 4.1 copy-start.16
  289.5 4.9 copy-start.17
  289.5 5.6 copy-start.18
  289.5 5.7 copy-start.19
  289.6 5.7 copy-start.20
  290.3 5.0 copy-start.21
  291.1 4.3 copy-start.22
  291.9 3.6 copy-start.23
  296.8 2.7 copy-start.6
  319.9 241.8 %all-to-all-start.2 = ((bf16[64,2,2,128,128]{4,3,2,1,0:T(8,128)(2,1)}), bf16[64,2,2,128,128]{4,3,2,1,0:T(8,128)(2,1)}, u32[]{:S(2)}, u32[]{:S(2)}) async-start(bf16[64,2,2,128,128]{4,3,2,1,0:T(8,128)(2,1)} %bitcast.313), calls=%async_computation.2 | async-start | bytes 16777216 | tf_op jit(solution)/shard_map/all_to_all | solution.py:134
  335.6 4.3 copy-start.13
  346.0 2.7 copy-start.9
  347.8 213.9 %collective-permute-start.11 = (bf16[2,4,2,128,128]{4,3,2,1,0:T(8,128)(2,1)}, bf16[2,4,2,128,128]{4,3,2,1,0:T(8,128)(2,1)S(1)}, u32[]{:S(2)}, u32[]{:S(2)}) collective-permute-start(bf16[2,4,2,128,128]{4,3,2,1,0:T(8,128)(2,1)} %get-tuple-element.13), channel_id=1, source_target_pairs={{0,16},{4,20},{8,24},{12,28},{16,0},{20,4},{24,8},{28,12},{32,48},... | collective-permute-start | bytes 1572872 | tf_op jit(solution)/shard_map/ppermute | solution.py:13
  350.7 219.2 %collective-permute-start.10 = (bf16[2,4,2,128,128]{4,3,2,1,0:T(8,128)(2,1)}, bf16[2,4,2,128,128]{4,3,2,1,0:T(8,128)(2,1)S(1)}, u32[]{:S(2)}, u32[]{:S(2)}) collective-permute-start(bf16[2,4,2,128,128]{4,3,2,1,0:T(8,128)(2,1)} %get-tuple-element.14), channel_id=1, source_target_pairs={{0,32},{4,36},{8,40},{12,44},{16,48},{20,52},{24,56},{28,60},{32,0... | collective-permute-start | bytes 1572872 | tf_op jit(solution)/shard_map/ppermute | solution.py:13
  352.7 217.1 %collective-permute-start.9 = (bf16[2,4,2,128,128]{4,3,2,1,0:T(8,128)(2,1)}, bf16[2,4,2,128,128]{4,3,2,1,0:T(8,128)(2,1)S(1)}, u32[]{:S(2)}, u32[]{:S(2)}) collective-permute-start(bf16[2,4,2,128,128]{4,3,2,1,0:T(8,128)(2,1)} %get-tuple-element.9), channel_id=1, source_target_pairs={{0,128},{4,132},{8,136},{12,140},{16,144},{20,148},{24,152},{28,15... | collective-permute-start | bytes 1572872 | tf_op jit(solution)/shard_map/ppermute | solution.py:13
  355.8 214.0 %collective-permute-start.8 = (bf16[2,4,2,128,128]{4,3,2,1,0:T(8,128)(2,1)}, bf16[2,4,2,128,128]{4,3,2,1,0:T(8,128)(2,1)}, u32[]{:S(2)}, u32[]{:S(2)}) collective-permute-start(bf16[2,4,2,128,128]{4,3,2,1,0:T(8,128)(2,1)} %get-tuple-element.10), channel_id=1, source_target_pairs={{0,64},{4,68},{8,72},{12,76},{16,80},{20,84},{24,88},{28,92},{32,9... | collective-permute-start | bytes 1572872 | tf_op jit(solution)/shard_map/ppermute | solution.py:13
  356.5 213.4 %collective-permute-start.7 = (bf16[2,4,2,128,128]{4,3,2,1,0:T(8,128)(2,1)}, bf16[2,4,2,128,128]{4,3,2,1,0:T(8,128)(2,1)}, u32[]{:S(2)}, u32[]{:S(2)}) collective-permute-start(bf16[2,4,2,128,128]{4,3,2,1,0:T(8,128)(2,1)} %get-tuple-element.11), channel_id=1, source_target_pairs={{0,8},{4,12},{8,0},{12,4},{16,24},{20,28},{24,16},{28,20},{32,40},... | collective-permute-start | bytes 1572872 | tf_op jit(solution)/shard_map/ppermute | solution.py:13
  561.7 8.2 %collective-permute-start.6 = (bf16[2,4,2,128,128]{4,3,2,1,0:T(8,128)(2,1)}, bf16[2,4,2,128,128]{4,3,2,1,0:T(8,128)(2,1)S(1)}, u32[]{:S(2)}, u32[]{:S(2)}) collective-permute-start(bf16[2,4,2,128,128]{4,3,2,1,0:T(8,128)(2,1)} %get-tuple-element.12), channel_id=1, source_target_pairs={{0,4},{4,0},{8,12},{12,8},{16,20},{20,16},{24,28},{28,24},{32,36},... | collective-permute-start | bytes 1572872 | tf_op jit(solution)/shard_map/ppermute | solution.py:13
  561.7 8.2 %copy-start.3 = (f32[1,4,2,8,128,128]{5,4,3,2,1,0:T(8,128)S(1)}, f32[1,4,2,8,128,128]{5,4,3,2,1,0:T(8,128)}, u32[]{:S(2)}) copy-start(f32[1,4,2,8,128,128]{5,4,3,2,1,0:T(8,128)} %copy-done.2) | copy-start | bytes 12582916
  561.7 8.3 %copy-start.5 = (f32[1,4,2,8,128,128]{5,4,3,2,1,0:T(8,128)S(1)}, f32[1,4,2,8,128,128]{5,4,3,2,1,0:T(8,128)}, u32[]{:S(2)}) copy-start(f32[1,4,2,8,128,128]{5,4,3,2,1,0:T(8,128)} %copy-done.4) | copy-start | bytes 12582916
  (10 other events, 16.6 us)
